TPU v7x, 32 devices: a whole 2x2x4 slice. The times are simulated.
32 devices in a mesh: group: 2 (over x), tm: 2 (over core), height: 8 (over z, y).
Axes of the slice: x: 2, y: 2, z: 4, core: 2. Of those that a mesh axis runs over, the one named last changes fastest.
Arguments:
- frames: bfloat16 [8, 16, 128, 384], P(('group', 'tm'), 'height'), parts along dimension 0, may hold values from -20 to 20
- earlier: int32 [8, 2], P(('group', 'tm')), parts along dimension 0, may hold values from -1 to 3, as said below
- gain_conv: float32 [384], replicated, may hold values from 0.1 to 1.9
- conv_weight: bfloat16 [3, 3, 3, 384, 384], replicated, may hold values from -0.0625 to 0.0625
- conv_bias: float32 [384], replicated, may hold values from -3 to 3
- gain_attn: float32 [384], replicated, may hold values from 0.1 to 1.9
- query_weight: bfloat16 [384, 384], replicated
- key_weight: bfloat16 [384, 384], replicated
- value_weight: bfloat16 [384, 384], replicated, may hold values from -0.3125 to 0.3125
- out_weight: bfloat16 [384, 384], replicated, may hold values from -0.3125 to 0.3125
Outputs:
- encoded: bfloat16 [8, 16, 128, 384], P(('group', 'tm'), 'height'), parts along dimension 0
There are 2 independent parts, one for each index of `group`. A program takes and returns all parts, laid end to end along the dimension named above; an argument that names none is the same for every part. Nothing has to cross between parts.
Inputs may be any that keep to these rules, and one draw needn't show every extreme that they name: Row i names the spans whose frames come two back and one back before span i's frame in the same clip, -1 where the clip has no such frame; spans of a clip may lie on either index of tm, in an order drawn from the seed. earlier[i, 0] is -1 whenever earlier[i, 1] is -1. Every span is named at most once in each column.
All inputs are finite; a program needn't handle non-finite values.
Results may differ from a plain program's by a relative error of at most 0.014.
Values may be sent and summed in bfloat16 or wider, within the bound.
No kernel may reach another device: no remote copies, remote signals or barrier semaphores. Data moves between devices by JAX's collectives and lax.ppermute only.
A program may use at most 128 MiB of HBM per device.

v0:
```python
import jax
import jax.numpy as jnp
from jax import lax
from jax.sharding import PartitionSpec as P


def padded_2(cells, sides, width):
    for axis, dim in sides:
        count = lax.axis_size(axis)
        ends = count - 1
        head = lax.slice_in_dim(cells, 0, width, axis=dim)
        tail = lax.slice_in_dim(cells, cells.shape[dim] - width, cells.shape[dim], axis=dim)
        cells = jnp.concatenate(
            [
                lax.ppermute(tail, axis, [(i, (i + 1) % count) for i in range(ends)]),
                cells,
                lax.ppermute(head, axis, [((i + 1) % count, i) for i in range(ends)]),
            ],
            axis=dim,
        )
    return cells


def rms_scaled(frames, gain):
    widened = frames.astype(jnp.float32)
    mean_square = jnp.mean(widened * widened, axis=-1, keepdims=True)
    return widened * lax.rsqrt(mean_square + 1e-06) * gain


def shards(
    frames,
    earlier,
    gain_conv,
    conv_weight,
    conv_bias,
    gain_attn,
    query_weight,
    key_weight,
    value_weight,
    out_weight,
):
    span_count, row_count, col_count, channels = frames.shape
    activated = jax.nn.silu(rms_scaled(frames, gain_conv)).astype(jnp.bfloat16)
    rimmed = padded_2(activated, (("height", 1),), 1)
    gathered = lax.all_gather(rimmed, "tm", axis=0, tiled=True)
    border = ((0, 0), (0, 0), (1, 1), (0, 0))
    padded = jnp.pad(rimmed, border)
    gathered = jnp.pad(gathered, border)
    back_two = jnp.take(gathered, jnp.maximum(earlier[:, 0], 0), axis=0)
    back_one = jnp.take(gathered, jnp.maximum(earlier[:, 1], 0), axis=0)
    present_two = (earlier[:, 0] >= 0)[:, None, None, None]
    present_one = (earlier[:, 1] >= 0)[:, None, None, None]
    back_two = jnp.where(present_two, back_two, jnp.zeros_like(back_two))
    back_one = jnp.where(present_one, back_one, jnp.zeros_like(back_one))
    window = jnp.stack([back_two, back_one, padded], axis=1)
    score_scale = 1.0 / channels**0.5

    def conv_span(span_window, span):
        accum = jnp.zeros((row_count, col_count, channels), jnp.float32)
        for tap_t in range(3):
            for tap_y in range(3):
                for tap_x in range(3):
                    sliced = span_window[
                        tap_t, tap_y : tap_y + row_count, tap_x : tap_x + col_count
                    ]
                    accum = accum + jnp.einsum(
                        "hwc,cd->hwd",
                        sliced,
                        conv_weight[tap_t, tap_y, tap_x],
                        preferred_element_type=jnp.float32,
                    )
        mixed = (frames[span].astype(jnp.float32) + accum + conv_bias).astype(jnp.bfloat16)
        normed = rms_scaled(mixed, gain_attn).astype(jnp.bfloat16)
        return (mixed, normed.reshape(row_count * col_count, channels))

    def attend_span(mixed, tokens, tokens_all):
        queries = jnp.dot(tokens, query_weight, preferred_element_type=jnp.float32).astype(
            jnp.bfloat16
        )
        keys_all = jnp.dot(tokens_all, key_weight, preferred_element_type=jnp.float32).astype(
            jnp.bfloat16
        )
        values_all = jnp.dot(tokens_all, value_weight, preferred_element_type=jnp.float32).astype(
            jnp.bfloat16
        )
        scores = (
            jnp.einsum("qc,kc->qk", queries, keys_all, preferred_element_type=jnp.float32)
            * score_scale
        )
        peaks = jnp.max(scores, axis=-1, keepdims=True)
        weights_exp = jnp.exp(scores - peaks)
        totals = jnp.sum(weights_exp, axis=-1, keepdims=True)
        summed = jnp.dot(
            weights_exp.astype(jnp.bfloat16), values_all, preferred_element_type=jnp.float32
        )
        attended = (summed / totals).astype(jnp.bfloat16)
        projected = jnp.dot(attended, out_weight, preferred_element_type=jnp.float32)
        encoded = mixed.astype(jnp.float32) + projected.reshape(row_count, col_count, channels)
        return encoded.astype(jnp.bfloat16)

    outputs = []
    pending = None
    span_window = window[0]
    for span in range(span_count):
        mixed, tokens = conv_span(span_window, span)
        if span + 1 < span_count:
            tokens, span_window = lax.optimization_barrier((tokens, window[span + 1]))
        tokens_all = lax.all_gather(tokens, "height", axis=0, tiled=True)
        if pending is not None:
            mixed, tokens, pending = lax.optimization_barrier((mixed, tokens, pending))
            outputs.append(attend_span(*pending))
        pending = (mixed, tokens, tokens_all)
    outputs.append(attend_span(*pending))
    return jnp.stack(outputs, axis=0)


def solution(mesh):
    in_specs = (
        P(("group", "tm"), "height", None, None),
        P(("group", "tm"), None),
        P(),
        P(),
        P(),
        P(),
        P(),
        P(),
        P(),
        P(),
    )
    out_specs = P(("group", "tm"), "height", None, None)
    return jax.shard_map(shards, mesh=mesh, in_specs=in_specs, out_specs=out_specs, check_vma=False)
```

profile of v0, /device:TPU:0, one launch (start us, length us, event | category | flops | bytes accessed | tf_op | source)
XLA Modules:
  0.0 183.2 jit_solution(11251715739805948440)
XLA Ops:
  7.8 1.3 fusion.29
  9.1 4.9 %collective-permute-start = (bf16[2,1,128,384]{3,2,1,0:T(8,128)(2,1)S(1)}, bf16[2,1,128,384]{3,2,1,0:T(8,128)(2,1)S(1)}, u32[]{:S(2)}, u32[]{:S(2)}) collective-permute-start(bf16[2,1,128,384]{3,2,1,0:T(8,128)(2,1)S(1)} %get-tuple-element.26), channel_id=1, source_target_pairs={{0,1},{1,2},{2,3},{3,4},{4,5},{5,6},{6,7},{8,9},{9,10},{10,11},{11... | collective-permute-start | bytes 589832 | tf_op jit(solution)/shard_map/ppermute | solution.py:15
  14.0 1.3 collective-permute-start.1
  15.3 2.9 %collective-permute-done = bf16[2,1,128,384]{3,2,1,0:T(8,128)(2,1)S(1)} collective-permute-done((bf16[2,1,128,384]{3,2,1,0:T(8,128)(2,1)S(1)}, bf16[2,1,128,384]{3,2,1,0:T(8,128)(2,1)S(1)}, u32[]{:S(2)}, u32[]{:S(2)}) %collective-permute-start) | collective-permute-done | bytes 196640 | tf_op jit(solution)/shard_map/ppermute | solution.py:15
  18.2 4.1 %collective-permute-done.1 = bf16[2,1,128,384]{3,2,1,0:T(8,128)(2,1)S(1)} collective-permute-done((bf16[2,1,128,384]{3,2,1,0:T(8,128)(2,1)S(1)}, bf16[2,1,128,384]{3,2,1,0:T(8,128)(2,1)S(1)}, u32[]{:S(2)}, u32[]{:S(2)}) %collective-permute-start.1) | collective-permute-done | bytes 196640 | tf_op jit(solution)/shard_map/ppermute | solution.py:17
  23.8 1.3 pad_bitcast_fusion
  25.1 10.4 %all-gather.4.cloned.1.call-done = bf16[4,4,128,384]{3,2,1,0:T(8,128)(2,1)} async-done(((bf16[2,4,128,384]{3,2,1,0:T(8,128)(2,1)}), bf16[4,4,128,384]{3,2,1,0:T(8,128)(2,1)}) %all-gather.4.cloned.1.call-update) | async-done | bytes 1572880 | tf_op jit(solution)/shard_map/all_gather | solution.py:45
  35.5 1.9 %pad.8 = bf16[4,4,130,384]{3,2,1,0:T(8,128)(2,1)S(1)} pad(bf16[4,4,128,384]{3,2,1,0:T(8,128)(2,1)} %all-gather.4.cloned.1.call-done, bf16[]{:T(256)} %constant.9.clone.1), padding=0_0x0_0x1_1x0_0 | pad | bytes 3170306 | tf_op jit(solution)/shard_map/jit(_pad)/pad | solution.py:48
  37.5 1.6 gather_fusion.1
  39.0 1.6 gather_fusion
  40.6 1.5 fusion.20
  42.9 1.5 fusion.38
  61.3 1.2 convolution_add_fusion.20
  62.5 1.2 convolution_add_fusion.19
  63.8 1.2 convolution_add_fusion.18
  68.7 1.2 convolution_add_fusion.14
  69.9 1.2 convolution_add_fusion.13
  71.2 1.2 convolution_add_fusion.12
  73.7 1.4 convolution_add_fusion.10
  76.4 1.2 convolution_add_fusion.8
  80.1 1.2 convolution_add_fusion.5
  81.4 1.2 convolution_add_fusion.4
  82.6 1.2 convolution_add_fusion.3
  83.9 1.3 convolution_add_fusion.2
  85.2 1.2 convolution_add_fusion.1
  86.4 1.4 fusion.33
  88.6 33.3 %all-gather.6.cloned.1.call-done = bf16[2048,384]{1,0:T(8,128)(2,1)} async-done(((bf16[256,384]{1,0:T(8,128)(2,1)}), bf16[2048,384]{1,0:T(8,128)(2,1)}) %all-gather.6.cloned.1.call-update) | async-done | bytes 1572880 | tf_op jit(solution)/shard_map/all_gather | solution.py:108
  122.2 3.1 %fusion.204 = (f32[256]{0:T(256)S(1)}, f32[256,2048]{1,0:T(8,128)S(1)}) fusion(bf16[256,384]{1,0:T(8,128)(2,1)S(1)} %convolution_convert_fusion.5, bf16[2048,384]{1,0:T(8,128)(2,1)} %all-gather.6.cloned.1.call-done, bf16[384,384]{1,0:T(8,128)(2,1)S(1)} %copy-done), kind=kOutput, calls=%fused_computation.322 | convolution fusion | flops 1008467712 | bytes 4162560 | tf_op jit(solution)/shard_map/qc,kc->qk/dot_general | solution.py:87
  127.2 3.1 %fusion.15 = bf16[256,384]{1,0:T(8,128)(2,1)S(1)} fusion(bf16[2048,384]{1,0:T(8,128)(2,1)} %all-gather.6.cloned.1.call-done, bf16[384,384]{1,0:T(8,128)(2,1)} %param.20, f32[256,2048]{1,0:T(8,128)S(1)} %get-tuple-element.35, f32[256]{0:T(256)S(1)} %get-tuple-element.34, f32[256]{0:T(256)S(1)} %fusion), kind=kOutput, calls=%fused_computation.82 | convolution fusion | flops 1008664576 | bytes 4163584 | tf_op jit(solution)/shard_map/dot_general | solution.py:93
  130.7 36.5 %all-gather.8.cloned.1.call-done = bf16[2048,384]{1,0:T(8,128)(2,1)} async-done(((bf16[256,384]{1,0:T(8,128)(2,1)}), bf16[2048,384]{1,0:T(8,128)(2,1)}) %all-gather.8.cloned.1.call-update) | async-done | bytes 1572880 | tf_op jit(solution)/shard_map/all_gather | solution.py:108
  167.1 3.3 %fusion.203 = (f32[256]{0:T(256)S(1)}, f32[256,2048]{1,0:T(8,128)S(1)}) fusion(bf16[256,384]{1,0:T(8,128)(2,1)} %convolution_convert_fusion.4, bf16[2048,384]{1,0:T(8,128)(2,1)} %all-gather.8.cloned.1.call-done, bf16[384,384]{1,0:T(8,128)(2,1)S(1)} %copy-done), kind=kOutput, calls=%fused_computation.321 | convolution fusion | flops 1008467712 | bytes 4162560 | tf_op jit(solution)/shard_map/qc,kc->qk/dot_general | solution.py:87
  170.8 3.8 %fusion.13 = bf16[256,384]{1,0:T(8,128)(2,1)} fusion(bf16[2048,384]{1,0:T(8,128)(2,1)} %all-gather.8.cloned.1.call-done, bf16[384,384]{1,0:T(8,128)(2,1)} %param.20, f32[256,2048]{1,0:T(8,128)S(1)} %get-tuple-element.33, f32[256]{0:T(256)S(1)} %get-tuple-element.32, f32[256]{0:T(256)S(1)} %fusion.2), kind=kOutput, calls=%fused_computation.80 | convolution fusion | flops 1008664576 | bytes 4163584 | tf_op jit(solution)/shard_map/dot_general | solution.py:93
  (96 shorter events, 34.4 us)
Async XLA Ops:
  6.5 115.6 %copy-start = (bf16[384,384]{1,0:T(8,128)(2,1)S(1)}, bf16[384,384]{1,0:T(8,128)(2,1)}, u32[]{:S(2)}) copy-start(bf16[384,384]{1,0:T(8,128)(2,1)} %param.19) | copy-start | bytes 884740
  6.5 16.8 %copy-start.7 = (s32[2,2]{1,0:T(2,128)S(1)}, s32[2,2]{1,0:T(2,128)}, u32[]{:S(2)}) copy-start(s32[2,2]{1,0:T(2,128)} %param.13) | copy-start | bytes 52
  6.5 29.0 %all-gather.4.cloned.1.call-start = ((), (), s32[]{:S(2)}) async-start(), calls=%async_computation | async-start | bytes 2359296 | tf_op jit(solution)/shard_map/all_gather | solution.py:45
  9.1 9.1 %collective-permute-start = (bf16[2,1,128,384]{3,2,1,0:T(8,128)(2,1)S(1)}, bf16[2,1,128,384]{3,2,1,0:T(8,128)(2,1)S(1)}, u32[]{:S(2)}, u32[]{:S(2)}) collective-permute-start(bf16[2,1,128,384]{3,2,1,0:T(8,128)(2,1)S(1)} %get-tuple-element.26), channel_id=1, source_target_pairs={{0,1},{1,2},{2,3},{3,4},{4,5},{5,6},{6,7},{8,9},{9,10},{10,11},{11... | collective-permute-start | bytes 589832 | tf_op jit(solution)/shard_map/ppermute | solution.py:15
  14.0 8.3 %collective-permute-start.1 = (bf16[2,1,128,384]{3,2,1,0:T(8,128)(2,1)S(1)}, bf16[2,1,128,384]{3,2,1,0:T(8,128)(2,1)S(1)}, u32[]{:S(2)}, u32[]{:S(2)}) collective-permute-start(bf16[2,1,128,384]{3,2,1,0:T(8,128)(2,1)S(1)} %get-tuple-element.27), channel_id=1, source_target_pairs={{1,0},{2,1},{3,2},{4,3},{5,4},{6,5},{7,6},{9,8},{10,9},{11,10},{12... | collective-permute-start | bytes 589832 | tf_op jit(solution)/shard_map/ppermute | solution.py:17
  23.3 98.6 %all-gather.6.cloned.1.call-start = ((), (), s32[]{:S(2)}) async-start(), calls=%async_computation.1 | async-start | bytes 1769472 | tf_op jit(solution)/shard_map/all_gather | solution.py:108
  40.6 1.5 copy-start.1
  40.6 5.1 %slice-start = ((s8[7962624]{0:T(1024)(128)(4,1)}), s8[4194304]{0:T(1024)(128)(4,1)S(1)}, s32[]{:S(2)}) async-start(s8[7962624]{0:T(1024)(128)(4,1)} %bitcast.403), calls=%async_computation.3 | async-start | bytes 8388608
  42.3 3.4 %slice-start.1 = ((s8[7962624]{0:T(1024)(128)(4,1)}), s8[3768320]{0:T(1024)(128)(4,1)S(1)}, s32[]{:S(2)}) async-start(s8[7962624]{0:T(1024)(128)(4,1)} %bitcast.403), calls=%async_computation.4 | async-start | bytes 7536640
  51.6 1.0 copy-start.4
  51.6 1.0 copy-start.9
  51.9 1.1 copy-start.8
  76.4 90.8 %all-gather.8.cloned.1.call-start = ((), (), s32[]{:S(2)}) async-start(), calls=%async_computation.2 | async-start | bytes 1769472 | tf_op jit(solution)/shard_map/all_gather | solution.py:108
  83.8 38.1 %copy-start.2 = (bf16[2,128,384]{2,1,0:T(8,128)(2,1)S(1)}, bf16[2,128,384]{2,1,0:T(8,128)(2,1)}, u32[]{:S(2)}) copy-start(bf16[2,128,384]{2,1,0:T(8,128)(2,1)} %fusion.32) | copy-start | bytes 589828
  83.8 38.1 %copy-start.6 = (bf16[384,384]{1,0:T(8,128)(2,1)S(1)}, bf16[384,384]{1,0:T(8,128)(2,1)}, u32[]{:S(2)}) copy-start(bf16[384,384]{1,0:T(8,128)(2,1)} %param.18) | copy-start | bytes 884740
  125.3 0.9 copy-start.3
  127.2 3.2 %copy-start.5 = (bf16[384,384]{1,0:T(8,128)(2,1)S(1)}, bf16[384,384]{1,0:T(8,128)(2,1)}, u32[]{:S(2)}) copy-start(bf16[384,384]{1,0:T(8,128)(2,1)} %param.21) | copy-start | bytes 884740
Sparse Core Ops, SparseCore 0:
  23.4 12.0 all-gather.3
  76.5 45.3 all-gather.5
  124.1 42.9 all-gather.7
where the time goes:
time: 185 us; the launch traced here: 183 us
  waiting for transfers between devices  87.1 us (47%)
  matrix products  59.4 us (32%)
  between operations  13.8 us (7%)
  other arithmetic  9.3 us (5%)
  local copies, waits for them, and re-layouts  7.41 us (4%)
  starting transfers between devices  6.26 us (3%)
    all_gather x2, waiting for transfers between devices, shards(): tokens_all = lax.all_gather(tokens, 'height', axis=0, tiled=True)  69.7 us
    dot_general x54, matrix products, conv_span(): jnp.einsum('hwc,cd->hwd', sliced, conv_weight[tap_t, tap_y, tap_x], prefe...  43.3 us
    all_gather x1, waiting for transfers between devices, shards(): gathered = lax.all_gather(rimmed, 'tm', axis=0, tiled=True)  10.4 us
    dot_general x2, matrix products, attend_span(): jnp.dot(weights_exp.astype(jnp.bfloat16), values_all, preferred_element_t...  6.95 us
    dot_general x2, matrix products, attend_span(): jnp.einsum('qc,kc->qk', queries, keys_all, preferred_element_type=jnp.flo...  6.41 us
    ppermute x1, starting transfers between devices, padded_2(): lax.ppermute(tail, axis, [(i, (i + 1) % count) for i in range(ends)])  4.88 us
    ppermute x1, waiting for transfers between devices, padded_2(): lax.ppermute(head, axis, [((i + 1) % count, i) for i in range(ends)])  4.07 us
  transfers between devices with their start and end apart: 5, of which 5 were waited for; matrix products, arithmetic and copies ran while one was open for 12% of the time, Pallas kernels for 0%

commit v1 on v0

--- a/solution.py
+++ b/solution.py
@@ -105,7 +105,25 @@
         mixed, tokens = conv_span(span_window, span)
         if span + 1 < span_count:
             tokens, span_window = lax.optimization_barrier((tokens, window[span + 1]))
-        tokens_all = lax.all_gather(tokens, "height", axis=0, tiled=True)
+        size, mine, span_2 = (lax.axis_size("height"), lax.axis_index("height"), tokens.shape[0])
+        right = [(i_2, (i_2 + 1) % size) for i_2 in range(size)]
+        left = [(i_2, (i_2 - 1) % size) for i_2 in range(size)]
+        tokens_all = jnp.zeros(
+            (*tokens.shape[:0], size * span_2, *tokens.shape[0 + 1 :]), tokens.dtype
+        )
+        tokens_all = lax.dynamic_update_slice_in_dim(tokens_all, tokens, mine * span_2, axis=0)
+        from_left = from_right = tokens
+        half = size // 2
+        for step in range(1, half + 1):
+            from_left = lax.ppermute(from_left, "height", right)
+            tokens_all = lax.dynamic_update_slice_in_dim(
+                tokens_all, from_left, (mine - step) % size * span_2, axis=0
+            )
+            if step < size - half:
+                from_right = lax.ppermute(from_right, "height", left)
+                tokens_all = lax.dynamic_update_slice_in_dim(
+                    tokens_all, from_right, (mine + step) % size * span_2, axis=0
+                )
         if pending is not None:
             mixed, tokens, pending = lax.optimization_barrier((mixed, tokens, pending))
             outputs.append(attend_span(*pending))

time: 185 us -> 146 us (0.79)
  waiting for transfers between devices: 87.1 us -> 33.1 us
  starting transfers between devices: 6.26 us -> 36.4 us
  matrix products: 59.4 us -> 31.6 us
  local copies, waits for them, and re-layouts: 7.41 us -> 22.2 us
    all_gather x2 -> x0, waiting for transfers between devices: 69.7 us -> none  [shards(): tokens_all = lax.all_gather(tokens, 'height', axis=0, tiled=True)]
    ppermute x0 -> x14, starting transfers between devices: none -> 30.3 us  [the longest x6 23.3 us: shards(): from_right = lax.ppermute(from_right, 'height', left)]
    dot_general x54, matrix products: 43.3 us -> 17.2 us  [conv_span(): jnp.einsum('hwc,cd->hwd', sliced, conv_weight[tap_t, tap_y, tap_x], prefe...]
    ppermute x0 -> x14, waiting for transfers between devices: none -> 15.2 us  [the longest x6 11.2 us: shards(): from_right = lax.ppermute(from_right, 'height', left)]
    dynamic_update_slice x0 -> x16, local copies, waits for them, and re-layouts: none -> 13 us  [the longest x8 7.47 us: shards(): lax.dynamic_update_slice_in_dim(tokens_all, from_left, (mine - step) % si...]
    another operation x0 -> x2, local copies, waits for them, and re-layouts: none -> 2.56 us
  transfers between devices with their start and end apart: 5 -> 17, of which waited for: 5 -> 8; matrix products, arithmetic and copies ran while one was open for 12% -> 21% of each run, Pallas kernels for 0% -> 0%
where the time goes in v1:
time: 146 us
  starting transfers between devices  36.4 us (25%)
  waiting for transfers between devices  33.1 us (23%)
  matrix products  31.6 us (22%)
  local copies, waits for them, and re-layouts  22.2 us (15%)
  between operations  14.2 us (10%)
  other arithmetic  7.93 us (5%)
    ppermute x6, starting transfers between devices, shards(): from_right = lax.ppermute(from_right, 'height', left)  23.3 us
    dot_general x54, matrix products, conv_span(): jnp.einsum('hwc,cd->hwd', sliced, conv_weight[tap_t, tap_y, tap_x], prefe...  17.2 us
    ppermute x6, waiting for transfers between devices, shards(): from_right = lax.ppermute(from_right, 'height', left)  11.2 us
    all_gather x1, waiting for transfers between devices, shards(): gathered = lax.all_gather(rimmed, 'tm', axis=0, tiled=True)  10.9 us
    dynamic_update_slice x8, local copies, waits for them, and re-layouts, shards(): lax.dynamic_update_slice_in_dim(tokens_all, from_left, (mine - step) % si...  7.47 us
    ppermute x8, starting transfers between devices, shards(): from_left = lax.ppermute(from_left, 'height', right)  6.92 us
    dot_general x2, matrix products, attend_span(): jnp.einsum('qc,kc->qk', queries, keys_all, preferred_element_type=jnp.flo...  6.42 us
    dot_general x2, matrix products, attend_span(): jnp.dot(weights_exp.astype(jnp.bfloat16), values_all, preferred_element_t...  6.27 us
  transfers between devices with their start and end apart: 17, of which 8 were waited for; matrix products, arithmetic and copies ran while one was open for 21% of the time, Pallas kernels for 0%

profile of v1, /device:TPU:0, one launch (start us, length us, event | category | flops | bytes accessed | tf_op | source)
XLA Modules:
  0.0 145.5 jit_solution(12430079028841573024)
XLA Ops:
  7.7 1.3 fusion.29
  9.1 4.9 %collective-permute-start = (bf16[2,1,128,384]{3,2,1,0:T(8,128)(2,1)S(1)}, bf16[2,1,128,384]{3,2,1,0:T(8,128)(2,1)S(1)}, u32[]{:S(2)}, u32[]{:S(2)}) collective-permute-start(bf16[2,1,128,384]{3,2,1,0:T(8,128)(2,1)S(1)} %get-tuple-element.26), channel_id=1, source_target_pairs={{0,1},{1,2},{2,3},{3,4},{4,5},{5,6},{6,7},{8,9},{9,10},{10,11},{11... | collective-permute-start | bytes 589832 | tf_op jit(solution)/shard_map/ppermute | solution.py:15
  14.0 1.3 collective-permute-start.1
  15.3 2.9 %collective-permute-done = bf16[2,1,128,384]{3,2,1,0:T(8,128)(2,1)S(1)} collective-permute-done((bf16[2,1,128,384]{3,2,1,0:T(8,128)(2,1)S(1)}, bf16[2,1,128,384]{3,2,1,0:T(8,128)(2,1)S(1)}, u32[]{:S(2)}, u32[]{:S(2)}) %collective-permute-start) | collective-permute-done | bytes 196640 | tf_op jit(solution)/shard_map/ppermute | solution.py:15
  18.2 4.1 %collective-permute-done.1 = bf16[2,1,128,384]{3,2,1,0:T(8,128)(2,1)S(1)} collective-permute-done((bf16[2,1,128,384]{3,2,1,0:T(8,128)(2,1)S(1)}, bf16[2,1,128,384]{3,2,1,0:T(8,128)(2,1)S(1)}, u32[]{:S(2)}, u32[]{:S(2)}) %collective-permute-start.1) | collective-permute-done | bytes 196640 | tf_op jit(solution)/shard_map/ppermute | solution.py:17
  24.6 10.9 %all-gather.2.cloned.1.call-done = bf16[4,4,128,384]{3,2,1,0:T(8,128)(2,1)} async-done(((bf16[2,4,128,384]{3,2,1,0:T(8,128)(2,1)}), bf16[4,4,128,384]{3,2,1,0:T(8,128)(2,1)}) %all-gather.2.cloned.1.call-update) | async-done | bytes 1572880 | tf_op jit(solution)/shard_map/all_gather | solution.py:45
  35.5 1.9 %pad.8 = bf16[4,4,130,384]{3,2,1,0:T(8,128)(2,1)S(1)} pad(bf16[4,4,128,384]{3,2,1,0:T(8,128)(2,1)} %all-gather.2.cloned.1.call-done, bf16[]{:T(256)} %constant.93.clone.1), padding=0_0x0_0x1_1x0_0 | pad | bytes 3170306 | tf_op jit(solution)/shard_map/jit(_pad)/pad | solution.py:48
  37.4 1.6 %gather_fusion.1 = bf16[2,4,130,384]{3,2,1,0:T(8,128)(2,1)} fusion(bf16[4,4,130,384]{3,2,1,0:T(8,128)(2,1)S(1)} %pad.8, s32[1024]{0:T(1024)S(1)} %pad_clamp_fusion), kind=kCustom, calls=%fused_computation.1.clone | custom fusion | bytes 1597448 | tf_op jit(solution)/shard_map/jit(_take)/gather | solution.py:50
  39.0 1.6 %gather_fusion = bf16[2,4,130,384]{3,2,1,0:T(8,128)(2,1)} fusion(bf16[4,4,130,384]{3,2,1,0:T(8,128)(2,1)S(1)} %pad.8, s32[1024]{0:T(1024)S(1)} %pad_clamp_fusion.1), kind=kCustom, calls=%fused_computation.clone | custom fusion | bytes 1597448 | tf_op jit(solution)/shard_map/jit(_take)/gather | solution.py:49
  40.6 1.5 %fusion.20 = bf16[2,1,4,130,384]{4,3,2,1,0:T(8,128)(2,1)S(1)} fusion(bf16[2,4,130,384]{3,2,1,0:T(8,128)(2,1)} %gather_fusion.1, pred[2]{0:T(512)(128)(4,1)S(1)} %get-tuple-element.38, pred[2]{0:T(512)(128)(4,1)S(1)} %get-tuple-element.21), kind=kLoop, calls=%fused_computation.88 | loop fusion | flops 798720 | bytes 1597444 | tf_op jit(solution)/shard_map/stack | solution.py:55
  42.9 1.5 %fusion.38 = f32[2,128,384]{2,1,0:T(8,128)S(1)} fusion(bf16[3,3,3,384,384]{4,3,2,1,0:T(8,128)(2,1)} %param.15, bf16[3,4,130,384]{3,2,1,0:T(8,128)(2,1)S(1)} %get-tuple-element.25), kind=kOutput, calls=%fused_computation.116 | convolution fusion | flops 75497472 | bytes 884736 | tf_op jit(solution)/shard_map/hwc,cd->hwd/dot_general | solution.py:66
  53.5 1.8 %collective-permute-start.2 = (bf16[256,384]{1,0:T(8,128)(2,1)S(1)}, bf16[256,384]{1,0:T(8,128)(2,1)S(1)}, u32[]{:S(2)}, u32[]{:S(2)}) collective-permute-start(bf16[256,384]{1,0:T(8,128)(2,1)S(1)} %bitcast.405), channel_id=1, source_target_pairs={{0,1},{1,2},{2,3},{3,4},{4,5},{5,6},{6,7},{7,0},{8,9},{9,10},{10,1... | collective-permute-start | bytes 589832 | tf_op jit(solution)/shard_map/ppermute | solution.py:118
  55.2 3.0 %collective-permute-start.3 = (bf16[256,384]{1,0:T(8,128)(2,1)S(1)}, bf16[256,384]{1,0:T(8,128)(2,1)S(1)}, u32[]{:S(2)}, u32[]{:S(2)}) collective-permute-start(bf16[256,384]{1,0:T(8,128)(2,1)S(1)} %bitcast.406), channel_id=1, source_target_pairs={{0,7},{1,0},{2,1},{3,2},{4,3},{5,4},{6,5},{7,6},{8,15},{9,8},{10,9... | collective-permute-start | bytes 589832 | tf_op jit(solution)/shard_map/ppermute | solution.py:123
  66.1 4.7 %collective-permute-start.10 = (bf16[256,384]{1,0:T(8,128)(2,1)S(1)}, bf16[256,384]{1,0:T(8,128)(2,1)S(1)}, u32[]{:S(2)}, u32[]{:S(2)}) collective-permute-start(bf16[256,384]{1,0:T(8,128)(2,1)S(1)} %bitcast.410), channel_id=1, source_target_pairs={{0,7},{1,0},{2,1},{3,2},{4,3},{5,4},{6,5},{7,6},{8,15},{9,8},{10,9... | collective-permute-start | bytes 589832 | tf_op jit(solution)/shard_map/ppermute | solution.py:123
  70.8 1.3 broadcast.101.clone.1
  72.8 1.3 broadcast.101.clone
  74.8 4.7 %collective-permute-start.5 = (bf16[256,384]{1,0:T(8,128)(2,1)S(1)}, bf16[256,384]{1,0:T(8,128)(2,1)S(1)}, u32[]{:S(2)}, u32[]{:S(2)}) collective-permute-start(bf16[256,384]{1,0:T(8,128)(2,1)S(1)} %collective-permute-done.3), channel_id=1, source_target_pairs={{0,7},{1,0},{2,1},{3,2},{4,3},{5,4},{6,5},{7,6},{8,15},{9,8},{10,9... | collective-permute-start | bytes 589832 | tf_op jit(solution)/shard_map/ppermute | solution.py:123
  79.6 2.5 %collective-permute-start.11 = (bf16[256,384]{1,0:T(8,128)(2,1)S(1)}, bf16[256,384]{1,0:T(8,128)(2,1)S(1)}, u32[]{:S(2)}, u32[]{:S(2)}) collective-permute-start(bf16[256,384]{1,0:T(8,128)(2,1)S(1)} %collective-permute-done.9), channel_id=1, source_target_pairs={{0,1},{1,2},{2,3},{3,4},{4,5},{5,6},{6,7},{7,0},{8,9},{9,10},{10,1... | collective-permute-start | bytes 589832 | tf_op jit(solution)/shard_map/ppermute | solution.py:118
  83.5 2.3 %collective-permute-start.12 = (bf16[256,384]{1,0:T(8,128)(2,1)S(1)}, bf16[256,384]{1,0:T(8,128)(2,1)S(1)}, u32[]{:S(2)}, u32[]{:S(2)}) collective-permute-start(bf16[256,384]{1,0:T(8,128)(2,1)S(1)} %collective-permute-done.10), channel_id=1, source_target_pairs={{0,7},{1,0},{2,1},{3,2},{4,3},{5,4},{6,5},{7,6},{8,15},{9,8},{10,9... | collective-permute-start | bytes 589832 | tf_op jit(solution)/shard_map/ppermute | solution.py:123
  87.2 4.0 %collective-permute-done.5 = bf16[256,384]{1,0:T(8,128)(2,1)S(1)} collective-permute-done((bf16[256,384]{1,0:T(8,128)(2,1)S(1)}, bf16[256,384]{1,0:T(8,128)(2,1)S(1)}, u32[]{:S(2)}, u32[]{:S(2)}) %collective-permute-start.5) | collective-permute-done | bytes 196640 | tf_op jit(solution)/shard_map/ppermute | solution.py:123
  91.1 4.3 %collective-permute-start.7 = (bf16[256,384]{1,0:T(8,128)(2,1)S(1)}, bf16[256,384]{1,0:T(8,128)(2,1)S(1)}, u32[]{:S(2)}, u32[]{:S(2)}) collective-permute-start(bf16[256,384]{1,0:T(8,128)(2,1)S(1)} %collective-permute-done.5), channel_id=1, source_target_pairs={{0,7},{1,0},{2,1},{3,2},{4,3},{5,4},{6,5},{7,6},{8,15},{9,8},{10,9... | collective-permute-start | bytes 589832 | tf_op jit(solution)/shard_map/ppermute | solution.py:123
  96.9 2.7 %collective-permute-done.12 = bf16[256,384]{1,0:T(8,128)(2,1)S(1)} collective-permute-done((bf16[256,384]{1,0:T(8,128)(2,1)S(1)}, bf16[256,384]{1,0:T(8,128)(2,1)S(1)}, u32[]{:S(2)}, u32[]{:S(2)}) %collective-permute-start.12) | collective-permute-done | bytes 196640 | tf_op jit(solution)/shard_map/ppermute | solution.py:123
  99.6 4.3 %collective-permute-start.14 = (bf16[256,384]{1,0:T(8,128)(2,1)S(1)}, bf16[256,384]{1,0:T(8,128)(2,1)S(1)}, u32[]{:S(2)}, u32[]{:S(2)}) collective-permute-start(bf16[256,384]{1,0:T(8,128)(2,1)S(1)} %collective-permute-done.12), channel_id=1, source_target_pairs={{0,7},{1,0},{2,1},{3,2},{4,3},{5,4},{6,5},{7,6},{8,15},{9,8},{10,9... | collective-permute-start | bytes 589832 | tf_op jit(solution)/shard_map/ppermute | solution.py:123
  105.3 3.9 %collective-permute-done.13 = bf16[256,384]{1,0:T(8,128)(2,1)} collective-permute-done((bf16[256,384]{1,0:T(8,128)(2,1)S(1)}, bf16[256,384]{1,0:T(8,128)(2,1)}, u32[]{:S(2)}, u32[]{:S(2)}) %collective-permute-start.13) | collective-permute-done | bytes 196640 | tf_op jit(solution)/shard_map/ppermute | solution.py:118
  109.1 2.6 %collective-permute-start.15 = (bf16[256,384]{1,0:T(8,128)(2,1)}, bf16[256,384]{1,0:T(8,128)(2,1)}, u32[]{:S(2)}, u32[]{:S(2)}) collective-permute-start(bf16[256,384]{1,0:T(8,128)(2,1)} %collective-permute-done.13), channel_id=1, source_target_pairs={{0,1},{1,2},{2,3},{3,4},{4,5},{5,6},{6,7},{7,0},{8,9},{9,10},{10,1... | collective-permute-start | bytes 589832 | tf_op jit(solution)/shard_map/ppermute | solution.py:118
  112.4 1.6 %constant_dynamic-update-slice_fusion.2 = bf16[2048,384]{1,0:T(8,128)(2,1)} fusion(bf16[2048,384]{1,0:T(8,128)(2,1)} %constant_dynamic-update-slice_fusion.3, bf16[256,384]{1,0:T(8,128)(2,1)} %collective-permute-done.13, s32[]{:T(128)S(6)} %select_n.103), kind=kLoop, calls=%fused_computation.311 | loop fusion | bytes 393220 | tf_op jit(solution)/shard_map/dynamic_update_slice | solution.py:119
  114.8 4.6 %collective-permute-done.14 = bf16[256,384]{1,0:T(8,128)(2,1)S(1)} collective-permute-done((bf16[256,384]{1,0:T(8,128)(2,1)S(1)}, bf16[256,384]{1,0:T(8,128)(2,1)S(1)}, u32[]{:S(2)}, u32[]{:S(2)}) %collective-permute-start.14) | collective-permute-done | bytes 196640 | tf_op jit(solution)/shard_map/ppermute | solution.py:123
  121.0 3.1 %fusion.204 = (f32[256]{0:T(256)S(1)}, f32[256,2048]{1,0:T(8,128)S(1)}) fusion(bf16[256,384]{1,0:T(8,128)(2,1)S(1)} %convolution_convert_fusion.5, bf16[2048,384]{1,0:T(8,128)(2,1)} %constant_dynamic-update-slice_fusion.8, bf16[384,384]{1,0:T(8,128)(2,1)S(1)} %copy-done), kind=kOutput, calls=%fused_computation.338 | convolution fusion | flops 1008467712 | bytes 4162560 | tf_op jit(solution)/shard_map/qc,kc->qk/dot_general | solution.py:87
  124.6 3.1 %fusion.15 = bf16[256,384]{1,0:T(8,128)(2,1)S(1)} fusion(bf16[2048,384]{1,0:T(8,128)(2,1)} %constant_dynamic-update-slice_fusion.8, bf16[384,384]{1,0:T(8,128)(2,1)} %param.20, f32[256,2048]{1,0:T(8,128)S(1)} %get-tuple-element.35, f32[256]{0:T(256)S(1)} %get-tuple-element.34, f32[256]{0:T(256)S(1)} %fusion), kind=kOutput, calls=%fused_computation.82 | convolution fusion | flops 1008664576 | bytes 4163584 | tf_op jit(solution)/shard_map/dot_general | solution.py:93
  128.7 1.6 %constant_dynamic-update-slice_fusion = bf16[2048,384]{1,0:T(8,128)(2,1)} fusion(bf16[2048,384]{1,0:T(8,128)(2,1)} %constant_dynamic-update-slice_fusion.1, bf16[256,384]{1,0:T(8,128)(2,1)} %collective-permute-done.15, s32[]{:T(128)S(6)} %select_n.107), kind=kLoop, calls=%fused_computation.309 | loop fusion | bytes 393220 | tf_op jit(solution)/shard_map/dynamic_update_slice | solution.py:119
  130.3 3.3 %fusion.203 = (f32[256]{0:T(256)S(1)}, f32[256,2048]{1,0:T(8,128)S(1)}) fusion(bf16[256,384]{1,0:T(8,128)(2,1)} %convolution_convert_fusion.4, bf16[2048,384]{1,0:T(8,128)(2,1)} %constant_dynamic-update-slice_fusion, bf16[384,384]{1,0:T(8,128)(2,1)S(1)} %copy-done), kind=kOutput, calls=%fused_computation.337 | convolution fusion | flops 1008467712 | bytes 4162560 | tf_op jit(solution)/shard_map/qc,kc->qk/dot_general | solution.py:87
  134.1 3.2 %fusion.13 = bf16[256,384]{1,0:T(8,128)(2,1)S(1)} fusion(bf16[2048,384]{1,0:T(8,128)(2,1)} %constant_dynamic-update-slice_fusion, bf16[384,384]{1,0:T(8,128)(2,1)} %param.20, f32[256,2048]{1,0:T(8,128)S(1)} %get-tuple-element.33, f32[256]{0:T(256)S(1)} %get-tuple-element.32, f32[256]{0:T(256)S(1)} %fusion.2), kind=kOutput, calls=%fused_computation.80 | convolution fusion | flops 1008664576 | bytes 4163584 | tf_op jit(solution)/shard_map/dot_general | solution.py:93
  (134 shorter events, 34.0 us)
Async XLA Ops:
  6.5 114.5 %copy-start = (bf16[384,384]{1,0:T(8,128)(2,1)S(1)}, bf16[384,384]{1,0:T(8,128)(2,1)}, u32[]{:S(2)}) copy-start(bf16[384,384]{1,0:T(8,128)(2,1)} %param.19) | copy-start | bytes 884740
  6.5 28.9 %all-gather.2.cloned.1.call-start = ((), (), s32[]{:S(2)}) async-start(), calls=%async_computation | async-start | bytes 2359296 | tf_op jit(solution)/shard_map/all_gather | solution.py:45
  9.1 14.4 %copy-start.6 = (s32[2,2]{1,0:T(2,128)S(1)}, s32[2,2]{1,0:T(2,128)}, u32[]{:S(2)}) copy-start(s32[2,2]{1,0:T(2,128)} %param.13) | copy-start | bytes 52
  9.1 9.1 %collective-permute-start = (bf16[2,1,128,384]{3,2,1,0:T(8,128)(2,1)S(1)}, bf16[2,1,128,384]{3,2,1,0:T(8,128)(2,1)S(1)}, u32[]{:S(2)}, u32[]{:S(2)}) collective-permute-start(bf16[2,1,128,384]{3,2,1,0:T(8,128)(2,1)S(1)} %get-tuple-element.26), channel_id=1, source_target_pairs={{0,1},{1,2},{2,3},{3,4},{4,5},{5,6},{6,7},{8,9},{9,10},{10,11},{11... | collective-permute-start | bytes 589832 | tf_op jit(solution)/shard_map/ppermute | solution.py:15
  14.0 8.3 %collective-permute-start.1 = (bf16[2,1,128,384]{3,2,1,0:T(8,128)(2,1)S(1)}, bf16[2,1,128,384]{3,2,1,0:T(8,128)(2,1)S(1)}, u32[]{:S(2)}, u32[]{:S(2)}) collective-permute-start(bf16[2,1,128,384]{3,2,1,0:T(8,128)(2,1)S(1)} %get-tuple-element.27), channel_id=1, source_target_pairs={{1,0},{2,1},{3,2},{4,3},{5,4},{6,5},{7,6},{9,8},{10,9},{11,10},{12... | collective-permute-start | bytes 589832 | tf_op jit(solution)/shard_map/ppermute | solution.py:17
  23.3 1.1 copy-start.1
  40.6 1.5 %copy-start.2 = (bf16[2,4,130,384]{3,2,1,0:T(8,128)(2,1)S(1)}, bf16[2,4,130,384]{3,2,1,0:T(8,128)(2,1)}, u32[]{:S(2)}) copy-start(bf16[2,4,130,384]{3,2,1,0:T(8,128)(2,1)} %gather_fusion) | copy-start | bytes 2396164
  40.6 5.1 %slice-start = ((s8[7962624]{0:T(1024)(128)(4,1)}), s8[4194304]{0:T(1024)(128)(4,1)S(1)}, s32[]{:S(2)}) async-start(s8[7962624]{0:T(1024)(128)(4,1)} %bitcast.403), calls=%async_computation.1 | async-start | bytes 8388608
  42.3 3.4 %slice-start.1 = ((s8[7962624]{0:T(1024)(128)(4,1)}), s8[3768320]{0:T(1024)(128)(4,1)S(1)}, s32[]{:S(2)}) async-start(s8[7962624]{0:T(1024)(128)(4,1)} %bitcast.403), calls=%async_computation.2 | async-start | bytes 7536640
  51.9 1.0 copy-start.3
  51.9 1.0 copy-start.8
  52.2 1.1 copy-start.7
  53.5 21.3 %collective-permute-start.2 = (bf16[256,384]{1,0:T(8,128)(2,1)S(1)}, bf16[256,384]{1,0:T(8,128)(2,1)S(1)}, u32[]{:S(2)}, u32[]{:S(2)}) collective-permute-start(bf16[256,384]{1,0:T(8,128)(2,1)S(1)} %bitcast.405), channel_id=1, source_target_pairs={{0,1},{1,2},{2,3},{3,4},{4,5},{5,6},{6,7},{7,0},{8,9},{9,10},{10,1... | collective-permute-start | bytes 589832 | tf_op jit(solution)/shard_map/ppermute | solution.py:118
  55.2 19.6 %collective-permute-start.3 = (bf16[256,384]{1,0:T(8,128)(2,1)S(1)}, bf16[256,384]{1,0:T(8,128)(2,1)S(1)}, u32[]{:S(2)}, u32[]{:S(2)}) collective-permute-start(bf16[256,384]{1,0:T(8,128)(2,1)S(1)} %bitcast.406), channel_id=1, source_target_pairs={{0,7},{1,0},{2,1},{3,2},{4,3},{5,4},{6,5},{7,6},{8,15},{9,8},{10,9... | collective-permute-start | bytes 589832 | tf_op jit(solution)/shard_map/ppermute | solution.py:123
  66.1 13.6 %collective-permute-start.9 = (bf16[256,384]{1,0:T(8,128)(2,1)S(1)}, bf16[256,384]{1,0:T(8,128)(2,1)S(1)}, u32[]{:S(2)}, u32[]{:S(2)}) collective-permute-start(bf16[256,384]{1,0:T(8,128)(2,1)S(1)} %bitcast.409), channel_id=1, source_target_pairs={{0,1},{1,2},{2,3},{3,4},{4,5},{5,6},{6,7},{7,0},{8,9},{9,10},{10,1... | collective-permute-start | bytes 589832 | tf_op jit(solution)/shard_map/ppermute | solution.py:118
  66.1 17.4 %collective-permute-start.10 = (bf16[256,384]{1,0:T(8,128)(2,1)S(1)}, bf16[256,384]{1,0:T(8,128)(2,1)S(1)}, u32[]{:S(2)}, u32[]{:S(2)}) collective-permute-start(bf16[256,384]{1,0:T(8,128)(2,1)S(1)} %bitcast.410), channel_id=1, source_target_pairs={{0,7},{1,0},{2,1},{3,2},{4,3},{5,4},{6,5},{7,6},{8,15},{9,8},{10,9... | collective-permute-start | bytes 589832 | tf_op jit(solution)/shard_map/ppermute | solution.py:123
  74.8 12.4 %collective-permute-start.4 = (bf16[256,384]{1,0:T(8,128)(2,1)S(1)}, bf16[256,384]{1,0:T(8,128)(2,1)S(1)}, u32[]{:S(2)}, u32[]{:S(2)}) collective-permute-start(bf16[256,384]{1,0:T(8,128)(2,1)S(1)} %collective-permute-done.2), channel_id=1, source_target_pairs={{0,1},{1,2},{2,3},{3,4},{4,5},{5,6},{6,7},{7,0},{8,9},{9,10},{10,1... | collective-permute-start | bytes 589832 | tf_op jit(solution)/shard_map/ppermute | solution.py:118
  74.8 16.3 %collective-permute-start.5 = (bf16[256,384]{1,0:T(8,128)(2,1)S(1)}, bf16[256,384]{1,0:T(8,128)(2,1)S(1)}, u32[]{:S(2)}, u32[]{:S(2)}) collective-permute-start(bf16[256,384]{1,0:T(8,128)(2,1)S(1)} %collective-permute-done.3), channel_id=1, source_target_pairs={{0,7},{1,0},{2,1},{3,2},{4,3},{5,4},{6,5},{7,6},{8,15},{9,8},{10,9... | collective-permute-start | bytes 589832 | tf_op jit(solution)/shard_map/ppermute | solution.py:123
  79.6 15.8 %collective-permute-start.11 = (bf16[256,384]{1,0:T(8,128)(2,1)S(1)}, bf16[256,384]{1,0:T(8,128)(2,1)S(1)}, u32[]{:S(2)}, u32[]{:S(2)}) collective-permute-start(bf16[256,384]{1,0:T(8,128)(2,1)S(1)} %collective-permute-done.9), channel_id=1, source_target_pairs={{0,1},{1,2},{2,3},{3,4},{4,5},{5,6},{6,7},{7,0},{8,9},{9,10},{10,1... | collective-permute-start | bytes 589832 | tf_op jit(solution)/shard_map/ppermute | solution.py:118
  83.5 16.0 %collective-permute-start.12 = (bf16[256,384]{1,0:T(8,128)(2,1)S(1)}, bf16[256,384]{1,0:T(8,128)(2,1)S(1)}, u32[]{:S(2)}, u32[]{:S(2)}) collective-permute-start(bf16[256,384]{1,0:T(8,128)(2,1)S(1)} %collective-permute-done.10), channel_id=1, source_target_pairs={{0,7},{1,0},{2,1},{3,2},{4,3},{5,4},{6,5},{7,6},{8,15},{9,8},{10,9... | collective-permute-start | bytes 589832 | tf_op jit(solution)/shard_map/ppermute | solution.py:123
  87.2 18.1 %collective-permute-start.6 = (bf16[256,384]{1,0:T(8,128)(2,1)S(1)}, bf16[256,384]{1,0:T(8,128)(2,1)S(1)}, u32[]{:S(2)}, u32[]{:S(2)}) collective-permute-start(bf16[256,384]{1,0:T(8,128)(2,1)S(1)} %collective-permute-done.4), channel_id=1, source_target_pairs={{0,1},{1,2},{2,3},{3,4},{4,5},{5,6},{6,7},{7,0},{8,9},{9,10},{10,1... | collective-permute-start | bytes 589832 | tf_op jit(solution)/shard_map/ppermute | solution.py:118
  91.1 22.9 %collective-permute-start.7 = (bf16[256,384]{1,0:T(8,128)(2,1)S(1)}, bf16[256,384]{1,0:T(8,128)(2,1)S(1)}, u32[]{:S(2)}, u32[]{:S(2)}) collective-permute-start(bf16[256,384]{1,0:T(8,128)(2,1)S(1)} %collective-permute-done.5), channel_id=1, source_target_pairs={{0,7},{1,0},{2,1},{3,2},{4,3},{5,4},{6,5},{7,6},{8,15},{9,8},{10,9... | collective-permute-start | bytes 589832 | tf_op jit(solution)/shard_map/ppermute | solution.py:123
  95.5 13.7 %collective-permute-start.13 = (bf16[256,384]{1,0:T(8,128)(2,1)S(1)}, bf16[256,384]{1,0:T(8,128)(2,1)}, u32[]{:S(2)}, u32[]{:S(2)}) collective-permute-start(bf16[256,384]{1,0:T(8,128)(2,1)S(1)} %collective-permute-done.11), channel_id=1, source_target_pairs={{0,1},{1,2},{2,3},{3,4},{4,5},{5,6},{6,7},{7,0},{8,9},{9,10},{10,1... | collective-permute-start | bytes 589832 | tf_op jit(solution)/shard_map/ppermute | solution.py:118
  96.2 24.6 %copy-start.5 = (bf16[384,384]{1,0:T(8,128)(2,1)S(1)}, bf16[384,384]{1,0:T(8,128)(2,1)}, u32[]{:S(2)}) copy-start(bf16[384,384]{1,0:T(8,128)(2,1)} %param.18) | copy-start | bytes 884740
  99.6 19.8 %collective-permute-start.14 = (bf16[256,384]{1,0:T(8,128)(2,1)S(1)}, bf16[256,384]{1,0:T(8,128)(2,1)S(1)}, u32[]{:S(2)}, u32[]{:S(2)}) collective-permute-start(bf16[256,384]{1,0:T(8,128)(2,1)S(1)} %collective-permute-done.12), channel_id=1, source_target_pairs={{0,7},{1,0},{2,1},{3,2},{4,3},{5,4},{6,5},{7,6},{8,15},{9,8},{10,9... | collective-permute-start | bytes 589832 | tf_op jit(solution)/shard_map/ppermute | solution.py:123
  105.3 14.8 %collective-permute-start.8 = (bf16[256,384]{1,0:T(8,128)(2,1)S(1)}, bf16[256,384]{1,0:T(8,128)(2,1)S(1)}, u32[]{:S(2)}, u32[]{:S(2)}) collective-permute-start(bf16[256,384]{1,0:T(8,128)(2,1)S(1)} %collective-permute-done.6), channel_id=1, source_target_pairs={{0,1},{1,2},{2,3},{3,4},{4,5},{5,6},{6,7},{7,0},{8,9},{9,10},{10,1... | collective-permute-start | bytes 589832 | tf_op jit(solution)/shard_map/ppermute | solution.py:118
  109.1 19.6 %collective-permute-start.15 = (bf16[256,384]{1,0:T(8,128)(2,1)}, bf16[256,384]{1,0:T(8,128)(2,1)}, u32[]{:S(2)}, u32[]{:S(2)}) collective-permute-start(bf16[256,384]{1,0:T(8,128)(2,1)} %collective-permute-done.13), channel_id=1, source_target_pairs={{0,1},{1,2},{2,3},{3,4},{4,5},{5,6},{6,7},{7,0},{8,9},{9,10},{10,1... | collective-permute-start | bytes 589832 | tf_op jit(solution)/shard_map/ppermute | solution.py:118
  134.0 3.2 %copy-start.4 = (bf16[384,384]{1,0:T(8,128)(2,1)S(1)}, bf16[384,384]{1,0:T(8,128)(2,1)}, u32[]{:S(2)}) copy-start(bf16[384,384]{1,0:T(8,128)(2,1)} %param.21) | copy-start | bytes 884740
Sparse Core Ops, SparseCore 0:
  23.4 12.0 all-gather.1
